TPU v7x, 128 devices: a whole 4x4x4 slice. The times are simulated.
128 devices in a mesh: row: 4 (over z_lo, core), col: 4 (over x), slab: 8 (over y, z_hi).
Axes of the slice: x: 4, y: 4, z: 4 (z_hi: 2, z_lo: 2; z = z_hi * 2 + z_lo), core: 2. Of those that a mesh axis runs over, the one named last changes fastest.
Arguments:
- amplitudes: bfloat16 [48, 48, 480, 128], P('row', 'col', 'slab'), may hold values from -6 to 6
- integrals: bfloat16 [48, 480, 48, 128], P('row', 'slab', 'col'), may hold values from -0.0625 to 0.0625
- irreps: int32 [19], replicated, may hold values from 0 to 1
- pair_mask: int32 [4, 4], replicated, may hold values 0 or 1
Outputs:
- cycle_term: bfloat16 [48, 48, 128, 128], P('row', 'col', 'slab')
Inputs may be any that keep to these rules, and one draw needn't show every extreme that they name: Each label is one of the two irreps of the point group. `pair_mask`: 1 marks a block pair whose amplitudes are kept.
All inputs are finite; a program needn't handle non-finite values.
Results may differ from a plain program's by a relative error of at most 0.001.
Values may be sent and summed in bfloat16 or wider, within the bound.
No kernel may reach another device: no remote copies, remote signals or barrier semaphores. Data moves between devices by JAX's collectives and lax.ppermute only.
A program may use at most 128 MiB of HBM per device.

v0:
```python
import jax
import jax.numpy as jnp
from jax import lax
from jax.sharding import PartitionSpec as P

OBLK = 12
VTILE = 32


def swapped(value, axis, stride):
    mask = 2**stride
    pairs = [(source, source ^ mask) for source in range(lax.axis_size(axis))]
    return lax.ppermute(value, axis, pairs)


def block_onehot(first_row, row_count, blocks, block_width):
    block_ids = (first_row + jnp.arange(row_count, dtype=jnp.int32)) // block_width
    return (block_ids[:, None] == jnp.arange(blocks, dtype=jnp.int32)[None, :]).astype(jnp.float32)


def contract(amp_piece, int_piece, i_start, k_start, pair_mask):
    i_rows = amp_piece.shape[0]
    k_count = amp_piece.shape[1]
    blocks = pair_mask.shape[0]
    factor = jnp.dot(
        jnp.dot(block_onehot(i_start, i_rows, blocks, OBLK), pair_mask.astype(jnp.float32)),
        block_onehot(k_start, k_count, blocks, OBLK).T,
    )
    masked = amp_piece * factor.astype(jnp.bfloat16)[:, :, None, None]
    return jnp.einsum("ikca,kcjb->ijab", masked, int_piece, preferred_element_type=jnp.float32)


def body(amplitudes, integrals, irreps, pair_mask):
    i_rows, k_rows, c_cols, win_cols = amplitudes.shape
    j_rows = integrals.shape[2]
    blocks = pair_mask.shape[0]
    row_at = lax.axis_index("row")
    col_at = lax.axis_index("col")
    slab_at = lax.axis_index("slab")
    i_start = row_at * i_rows
    occ_labels = irreps[:blocks].astype(jnp.float32)
    vir_labels = irreps[blocks:].astype(jnp.float32)
    vir_tiles = vir_labels.shape[0]
    label_k = jnp.dot(
        block_onehot(row_at * integrals.shape[0], integrals.shape[0], blocks, OBLK), occ_labels
    )
    label_c = jnp.dot(block_onehot(slab_at * c_cols, c_cols, vir_tiles, VTILE), vir_labels)
    label_j = jnp.dot(block_onehot(col_at * j_rows, j_rows, blocks, OBLK), occ_labels)
    label_b = jnp.dot(block_onehot(0, win_cols, vir_tiles, VTILE), vir_labels)
    parity = (
        label_k[:, None, None, None]
        + label_c[None, :, None, None]
        + label_j[None, None, :, None]
        + label_b[None, None, None, :]
    )
    screened = jnp.where(jnp.remainder(parity, 2.0) == 0.0, integrals, jnp.zeros_like(integrals))
    int_whole = lax.all_gather(screened, "row", axis=0, tiled=True)
    cycle_part = contract(
        lax.all_gather(amplitudes, "col", axis=1, tiled=True),
        int_whole,
        i_start,
        jnp.int32(0),
        pair_mask,
    )
    shares = lax.psum_scatter(cycle_part, "slab", scatter_dimension=2, tiled=True)
    spread = lax.all_to_all(shares, "slab", split_axis=3, concat_axis=2, tiled=True)
    mirrored = jnp.transpose(spread, (1, 0, 3, 2))
    for bit_no in range(lax.axis_size("row").bit_length() - 1):
        across = swapped(swapped(mirrored, "row", bit_no), "col", bit_no)
        differ = row_at // 2**bit_no % 2 != col_at // 2**bit_no % 2
        mirrored = jnp.where(differ, across, mirrored)
    return (shares + mirrored).astype(jnp.bfloat16)


def solution(mesh):
    return jax.shard_map(
        body,
        mesh=mesh,
        in_specs=(P("row", "col", "slab", None), P("row", "slab", "col", None), P(), P()),
        out_specs=P("row", "col", "slab", None),
        check_vma=False,
    )
```

profile of v0, /device:TPU:0, one launch (start us, length us, event | category | flops | bytes accessed | tf_op | source)
XLA Modules:
  0.0 556.6 jit_solution(18274877579923600509)
XLA Ops:
  6.5 0.7 all-gather.5.cloned.1.call-update
  8.4 5.2 fusion.9
  13.7 0.6 copy-done.1
  14.6 88.8 %all-gather.5.cloned.1.call-done = bf16[12,48,60,128]{3,2,1,0:T(8,128)(2,1)} async-done(((bf16[12,12,60,128]{3,2,1,0:T(8,128)(2,1)}), bf16[12,48,60,128]{3,2,1,0:T(8,128)(2,1)}) %all-gather.5.cloned.1.call-update) | async-done | bytes 8847376 | tf_op jit(solution)/shard_map/all_gather | solution.py:59
  103.4 91.3 %all-gather.3.cloned.1.call-done = bf16[48,60,12,128]{3,1,0,2:T(8,128)(2,1)} async-done(((bf16[12,60,12,128]{3,1,0,2:T(8,128)(2,1)}), bf16[48,60,12,128]{3,1,0,2:T(8,128)(2,1)}) %all-gather.3.cloned.1.call-update) | async-done | bytes 8847376 | tf_op jit(solution)/shard_map/all_gather | solution.py:57
  194.7 21.9 %fusion.10 = f32[12,12,128,128]{2,3,0,1:T(8,128)} fusion(bf16[12,48,60,128]{3,2,1,0:T(8,128)(2,1)} %all-gather.5.cloned.1.call-done, bf16[12,48]{1,0:T(8,128)(2,1)S(1)} %convolution_convert_fusion, bf16[48,60,12,128]{3,1,0,2:T(8,128)(2,1)} %all-gather.3.cloned.1.call-done), kind=kOutput, calls=%fused_computation.13 | convolution fusion | flops 13607239680 | bytes 27133056 | tf_op jit(solution)/shard_map/ikca,kcjb->ijab/dot_general | solution.py:30
  216.6 12.7 %copy.18 = f32[12,12,128,128]{3,1,0,2:T(8,128)} copy(f32[12,12,128,128]{2,3,0,1:T(8,128)} %fusion.10) | data formatting | bytes 18874368 | tf_op jit(solution)/shard_map/ikca,kcjb->ijab/transpose | solution.py:30
  229.3 153.7 %reduce-scatter.2.cloned.1.call-done = f32[12,12,16,128]{3,1,0,2:T(8,128)} async-done(((f32[12,12,128,128]{3,1,0,2:T(8,128)}), f32[12,12,16,128]{3,1,0,2:T(8,128)}) %reduce-scatter.2.cloned.1.call-update) | async-done | bytes 1179664 | tf_op jit(solution)/shard_map/reduce_scatter | solution.py:65
  383.1 14.2 %copy.19 = f32[12,12,16,128]{2,0,1,3:T(8,128)} copy(f32[12,12,16,128]{3,1,0,2:T(8,128)} %reduce-scatter.2.cloned.1.call-done) | data formatting | bytes 2359296 | tf_op jit(solution)/shard_map/reduce_scatter | solution.py:65
  397.3 8.8 %reshape.121 = f32[8,1,36864]{2,1,0:T(1,128)S(1)} reshape(f32[128,12,12,16]{3,2,1,0:T(8,128)} %bitcast.47) | data formatting | bytes 2359296
  406.1 20.4 %all_to_all.18 = f32[8,1,36864]{2,1,0:T(1,128)S(1)} all-to-all(f32[8,1,36864]{2,1,0:T(1,128)S(1)} %reshape.121), channel_id=1, replica_groups=mesh['row'=4,'col'=4,'slab'=8] {'slab'}, dimensions={0} | all-to-all | bytes 2359296 | tf_op jit(solution)/shard_map/all_to_all | solution.py:66
  427.0 3.4 reduce
  430.5 10.0 %reshape.122 = f32[128,12,12,16]{3,2,1,0:T(8,128)} reshape(f32[8,36864]{1,0:T(8,128)S(1)} %reduce) | data formatting | bytes 2359296
  440.5 13.8 %copy.38 = f32[12,12,16,8,16]{2,3,4,1,0:T(8,128)} copy(f32[12,12,16,8,16]{2,0,1,4,3:T(8,128)} %bitcast.48) | data formatting | bytes 2359296 | tf_op jit(solution)/shard_map/all_to_all | solution.py:66
  454.3 6.2 %all_to_all.16 = f32[12,12,128,16]{2,3,1,0:T(8,128)S(1)} reshape(f32[12,12,8,16,16]{3,2,4,1,0:T(8,128)} %bitcast.49) | data formatting | bytes 2359296 | tf_op jit(solution)/shard_map/all_to_all | solution.py:66
  460.8 2.8 collective-permute-done
  463.6 1.5 collective-permute-start.1
  465.1 26.5 %collective-permute-done.1 = f32[12,12,16,128]{3,2,1,0:T(8,128)S(1)} collective-permute-done((f32[12,12,16,128]{3,2,1,0:T(8,128)S(1)}, f32[12,12,16,128]{3,2,1,0:T(8,128)S(1)}, u32[]{:S(2)}, u32[]{:S(2)}) %collective-permute-start.1) | collective-permute-done | bytes 1179680 | tf_op jit(solution)/shard_map/ppermute | solution.py:13
  491.9 1.3 collective-permute-start.2
  493.2 25.9 %collective-permute-done.2 = f32[12,12,16,128]{3,2,1,0:T(8,128)S(1)} collective-permute-done((f32[12,12,16,128]{3,2,1,0:T(8,128)S(1)}, f32[12,12,16,128]{3,2,1,0:T(8,128)S(1)}, u32[]{:S(2)}, u32[]{:S(2)}) %collective-permute-start.2) | collective-permute-done | bytes 1179680 | tf_op jit(solution)/shard_map/ppermute | solution.py:13
  519.1 3.0 collective-permute-start.3
  522.1 24.8 %collective-permute-done.3 = f32[12,12,16,128]{3,2,1,0:T(8,128)S(1)} collective-permute-done((f32[12,12,16,128]{3,2,1,0:T(8,128)S(1)}, f32[12,12,16,128]{3,2,1,0:T(8,128)S(1)}, u32[]{:S(2)}, u32[]{:S(2)}) %collective-permute-start.3) | collective-permute-done | bytes 1179680 | tf_op jit(solution)/shard_map/ppermute | solution.py:13
  546.9 2.2 fusion.15
  549.1 1.0 copy.26
  (27 shorter events, 2.5 us)
Async XLA Ops:
  6.5 0.9 copy-start.2
  6.5 1.8 copy-start
  6.5 96.9 %all-gather.5.cloned.1.call-start = ((), (), s32[]{:S(2)}) async-start(), calls=%async_computation.3 | async-start | bytes 11796480 | tf_op jit(solution)/shard_map/all_gather | solution.py:59
  7.3 187.4 %all-gather.3.cloned.1.call-start = ((), (), s32[]{:S(2)}) async-start(), calls=%async_computation.2 | async-start | bytes 11796480 | tf_op jit(solution)/shard_map/all_gather | solution.py:57
  13.6 0.7 copy-start.1
  13.6 369.5 %reduce-scatter.2.cloned.1.call-start = ((), (), s32[]{:S(2)}) async-start(), calls=%async_computation.4 | async-start | bytes 14155776 | tf_op jit(solution)/shard_map/reduce_scatter | solution.py:65
  460.7 2.9 collective-permute-start
  463.6 28.0 %collective-permute-start.1 = (f32[12,12,16,128]{3,2,1,0:T(8,128)S(1)}, f32[12,12,16,128]{3,2,1,0:T(8,128)S(1)}, u32[]{:S(2)}, u32[]{:S(2)}) collective-permute-start(f32[12,12,16,128]{3,2,1,0:T(8,128)S(1)} %collective-permute-done), channel_id=1, source_target_pairs={{0,8},{8,0},{16,24},{24,16},{1,9},{9,1},{17,25},{25,17},{2,10},{10... | collective-permute-start | bytes 3538952 | tf_op jit(solution)/shard_map/ppermute | solution.py:13
  491.9 27.2 %collective-permute-start.2 = (f32[12,12,16,128]{3,2,1,0:T(8,128)S(1)}, f32[12,12,16,128]{3,2,1,0:T(8,128)S(1)}, u32[]{:S(2)}, u32[]{:S(2)}) collective-permute-start(f32[12,12,16,128]{3,2,1,0:T(8,128)S(1)} %copy.23), channel_id=1, source_target_pairs={{0,64},{32,96},{64,0},{96,32},{1,65},{33,97},{65,1},{97,33},{2,66}... | collective-permute-start | bytes 3538952 | tf_op jit(solution)/shard_map/ppermute | solution.py:13
  519.1 27.8 %collective-permute-start.3 = (f32[12,12,16,128]{3,2,1,0:T(8,128)S(1)}, f32[12,12,16,128]{3,2,1,0:T(8,128)S(1)}, u32[]{:S(2)}, u32[]{:S(2)}) collective-permute-start(f32[12,12,16,128]{3,2,1,0:T(8,128)S(1)} %collective-permute-done.2), channel_id=1, source_target_pairs={{0,16},{8,24},{16,0},{24,8},{1,17},{9,25},{17,1},{25,9},{2,18},{10... | collective-permute-start | bytes 3538952 | tf_op jit(solution)/shard_map/ppermute | solution.py:13
Sparse Core Ops, SparseCore 0:
  9.0 94.3 all-gather.4
  105.1 89.5 all-gather.2
  229.4 153.5 reduce-scatter.1
where the time goes:
time: 557 us
  waiting for transfers between devices  415 us (75%)
  local copies, waits for them, and re-layouts  68.1 us (12%)
  matrix products  23.1 us (4%)
  blocking collectives  20.4 us (4%)
  between operations  13.2 us (2%)
  other arithmetic  11.2 us (2%)
  starting transfers between devices  6.01 us (1%)
    reduce_scatter x1, waiting for transfers between devices, body(): lax.psum_scatter(cycle_part, 'slab', scatter_dimension=2, tiled=True)  154 us
    all_gather x1, waiting for transfers between devices, body(): int_whole = lax.all_gather(screened, 'row', axis=0, tiled=True)  91.3 us
    all_gather x1, waiting for transfers between devices, body(): lax.all_gather(amplitudes, 'col', axis=1, tiled=True)  88.8 us
    ppermute x4, waiting for transfers between devices, swapped(): return lax.ppermute(value, axis, pairs)  80 us
    dot_general x1, matrix products, contract(): jnp.einsum('ikca,kcjb->ijab', masked, int_piece, preferred_element_type=j...  21.9 us
    all_to_all x3, local copies, waits for them, and re-layouts, body(): lax.all_to_all(shares, 'slab', split_axis=3, concat_axis=2, tiled=True)  20.5 us
    all_to_all x1, blocking collectives, body(): lax.all_to_all(shares, 'slab', split_axis=3, concat_axis=2, tiled=True)  20.4 us
    unnamed x8, local copies, waits for them, and re-layouts  19.5 us
  transfers between devices with their start and end apart: 7, of which 7 were waited for; matrix products, arithmetic and copies ran while one was open for 1% of the time, Pallas kernels for 0%

commit v1 on v0

--- a/solution.py
+++ b/solution.py
@@ -5,6 +5,19 @@
 
 OBLK = 12
 VTILE = 32
+
+
+def ring_gather(x, axis, dim):
+    ways = lax.axis_size(axis)
+    up = [(d, (d + 1) % ways) for d in range(ways)]
+    down = [(d, (d - 1) % ways) for d in range(ways)]
+    earlier, later = ([x], [x])
+    for _ in range(ways // 2):
+        earlier.append(lax.ppermute(earlier[-1], axis, up))
+    for _ in range((ways - 1) // 2):
+        later.append(lax.ppermute(later[-1], axis, down))
+    line = jnp.concatenate([*earlier[::-1], *later[1:]], axis=dim)
+    return jnp.roll(line, (lax.axis_index(axis) - ways // 2) * x.shape[dim], axis=dim)
 
 
 def swapped(value, axis, stride):
@@ -56,11 +69,7 @@
     screened = jnp.where(jnp.remainder(parity, 2.0) == 0.0, integrals, jnp.zeros_like(integrals))
     int_whole = lax.all_gather(screened, "row", axis=0, tiled=True)
     cycle_part = contract(
-        lax.all_gather(amplitudes, "col", axis=1, tiled=True),
-        int_whole,
-        i_start,
-        jnp.int32(0),
-        pair_mask,
+        ring_gather(amplitudes, "col", 1), int_whole, i_start, jnp.int32(0), pair_mask
     )
     shares = lax.psum_scatter(cycle_part, "slab", scatter_dimension=2, tiled=True)
     spread = lax.all_to_all(shares, "slab", split_axis=3, concat_axis=2, tiled=True)

time: 557 us -> 512 us (0.919)
  waiting for transfers between devices: 415 us -> 335 us
  local copies, waits for them, and re-layouts: 68.1 us -> 93.7 us
    ppermute x0 -> x3, waiting for transfers between devices: none -> 103 us  [the longest x2 103 us: ring_gather(): earlier.append(lax.ppermute(earlier[-1], axis, up))]
    all_gather x1, waiting for transfers between devices: 91.3 us -> 0.01 us  [body(): int_whole = lax.all_gather(screened, 'row', axis=0, tiled=True)]
    all_gather x1 -> x0, waiting for transfers between devices: 88.8 us -> none  [body(): lax.all_gather(amplitudes, 'col', axis=1, tiled=True)]
    unnamed x8 -> x13, local copies, waits for them, and re-layouts: 19.5 us -> 41.5 us
  transfers between devices with their start and end apart: 7 -> 9, of which waited for: 7 -> 7; matrix products, arithmetic and copies ran while one was open for 1% -> 5% of each run, Pallas kernels for 0% -> 0%
where the time goes in v1:
time: 512 us; the launch traced here: 511 us
  waiting for transfers between devices  335 us (65%)
  local copies, waits for them, and re-layouts  93.7 us (18%)
  matrix products  25.9 us (5%)
  blocking collectives  20.4 us (4%)
  between operations  13.5 us (3%)
  other arithmetic  12.4 us (2%)
  starting transfers between devices  10.8 us (2%)
    reduce_scatter x1, waiting for transfers between devices, body(): lax.psum_scatter(cycle_part, 'slab', scatter_dimension=2, tiled=True)  152 us
    ppermute x2, waiting for transfers between devices, ring_gather(): earlier.append(lax.ppermute(earlier[-1], axis, up))  103 us
    ppermute x4, waiting for transfers between devices, swapped(): return lax.ppermute(value, axis, pairs)  80.1 us
    unnamed x13, local copies, waits for them, and re-layouts  41.5 us
    dot_general x1, matrix products, contract(): jnp.einsum('ikca,kcjb->ijab', masked, int_piece, preferred_element_type=j...  22 us
    all_to_all x3, local copies, waits for them, and re-layouts, body(): lax.all_to_all(shares, 'slab', split_axis=3, concat_axis=2, tiled=True)  20.6 us
    all_to_all x1, blocking collectives, body(): lax.all_to_all(shares, 'slab', split_axis=3, concat_axis=2, tiled=True)  20.4 us
    reduce_scatter x1, local copies, waits for them, and re-layouts, body(): lax.psum_scatter(cycle_part, 'slab', scatter_dimension=2, tiled=True)  14.2 us
  transfers between devices with their start and end apart: 9, of which 7 were waited for; matrix products, arithmetic and copies ran while one was open for 5% of the time, Pallas kernels for 0%

profile of v1, /device:TPU:0, one launch (start us, length us, event | category | flops | bytes accessed | tf_op | source)
XLA Modules:
  0.0 511.2 jit_solution(4302197141617056113)
XLA Ops:
  10.4 6.4 %fusion.10 = bf16[12,60,12,128]{3,1,0,2:T(8,128)(2,1)} fusion(bf16[12,60,12,128]{3,1,2,0:T(8,128)(2,1)} %param.5, f32[128]{0:T(128)S(1)} %convolution_bitcast_fusion, f32[12,60,12]{1,0,2:T(8,128)S(1)} %broadcast_add_fusion), kind=kLoop, calls=%fused_computation.13 | loop fusion | flops 9953280 | bytes 4458752 | tf_op jit(solution)/shard_map/jit(_where)/select_n | solution.py:69
  18.5 52.6 %collective-permute-done = bf16[12,12,60,128]{3,2,1,0:T(8,128)(2,1)} collective-permute-done((bf16[12,12,60,128]{3,2,1,0:T(8,128)(2,1)S(1)}, bf16[12,12,60,128]{3,2,1,0:T(8,128)(2,1)}, u32[]{:S(2)}, u32[]{:S(2)}) %collective-permute-start) | collective-permute-done | bytes 2211872 | tf_op jit(solution)/shard_map/ppermute | solution.py:16
  74.8 50.0 %collective-permute-done.1 = bf16[12,12,60,128]{3,2,1,0:T(8,128)(2,1)} collective-permute-done((bf16[12,12,60,128]{3,2,1,0:T(8,128)(2,1)}, bf16[12,12,60,128]{3,2,1,0:T(8,128)(2,1)}, u32[]{:S(2)}, u32[]{:S(2)}) %collective-permute-start.1) | collective-permute-done | bytes 2211872 | tf_op jit(solution)/shard_map/ppermute | solution.py:16
  124.7 3.5 constant_dynamic-update-slice_fusion.7
  128.3 3.6 constant_dynamic-update-slice_fusion.6
  134.2 3.6 constant_dynamic-update-slice_fusion.4
  137.8 3.6 constant_dynamic-update-slice_fusion.3
  141.3 3.7 constant_dynamic-update-slice_fusion.2
  147.4 3.6 constant_dynamic-update-slice_fusion
  151.0 22.0 %fusion.11 = f32[12,12,128,128]{2,3,0,1:T(8,128)} fusion(bf16[12,96,60,128]{3,2,1,0:T(8,128)(2,1)} %constant_dynamic-update-slice_fusion, s32[]{:T(128)S(6)} %select_n.113, bf16[12,48]{1,0:T(8,128)(2,1)S(1)} %convolution_convert_fusion, bf16[48,60,12,128]{3,1,0,2:T(8,128)(2,1)} %all-gather.2.cloned.1.call-done), kind=kOutput, calls=%fused_computation.14 | convolution fusion | flops 13607239680 | bytes 28312708 | tf_op jit(solution)/shard_map/ikca,kcjb->ijab/dot_general | solution.py:43
  172.9 12.7 %copy.18 = f32[12,12,128,128]{3,1,0,2:T(8,128)} copy(f32[12,12,128,128]{2,3,0,1:T(8,128)} %fusion.11) | data formatting | bytes 18874368 | tf_op jit(solution)/shard_map/ikca,kcjb->ijab/transpose | solution.py:43
  185.6 151.7 %reduce-scatter.2.cloned.1.call-done = f32[12,12,16,128]{3,1,0,2:T(8,128)} async-done(((f32[12,12,128,128]{3,1,0,2:T(8,128)}), f32[12,12,16,128]{3,1,0,2:T(8,128)}) %reduce-scatter.2.cloned.1.call-update) | async-done | bytes 1179664 | tf_op jit(solution)/shard_map/reduce_scatter | solution.py:74
  337.4 14.2 %copy.19 = f32[12,12,16,128]{2,0,1,3:T(8,128)} copy(f32[12,12,16,128]{3,1,0,2:T(8,128)} %reduce-scatter.2.cloned.1.call-done) | data formatting | bytes 2359296 | tf_op jit(solution)/shard_map/reduce_scatter | solution.py:74
  351.6 8.8 %reshape.121 = f32[8,1,36864]{2,1,0:T(1,128)S(1)} reshape(f32[128,12,12,16]{3,2,1,0:T(8,128)} %bitcast.47) | data formatting | bytes 2359296
  360.4 20.4 %all_to_all.18 = f32[8,1,36864]{2,1,0:T(1,128)S(1)} all-to-all(f32[8,1,36864]{2,1,0:T(1,128)S(1)} %reshape.121), channel_id=1, replica_groups=mesh['row'=4,'col'=4,'slab'=8] {'slab'}, dimensions={0} | all-to-all | bytes 2359296 | tf_op jit(solution)/shard_map/all_to_all | solution.py:75
  381.3 3.4 reduce
  384.7 10.0 %reshape.122 = f32[128,12,12,16]{3,2,1,0:T(8,128)} reshape(f32[8,36864]{1,0:T(8,128)S(1)} %reduce) | data formatting | bytes 2359296
  394.8 13.8 %copy.38 = f32[12,12,16,8,16]{2,3,4,1,0:T(8,128)} copy(f32[12,12,16,8,16]{2,0,1,4,3:T(8,128)} %bitcast.48) | data formatting | bytes 2359296 | tf_op jit(solution)/shard_map/all_to_all | solution.py:75
  408.6 6.2 %all_to_all.16 = f32[12,12,128,16]{2,3,1,0:T(8,128)S(1)} reshape(f32[12,12,8,16,16]{3,2,4,1,0:T(8,128)} %bitcast.49) | data formatting | bytes 2359296 | tf_op jit(solution)/shard_map/all_to_all | solution.py:75
  415.1 2.8 collective-permute-done.3
  419.4 26.5 %collective-permute-done.4 = f32[12,12,16,128]{3,2,1,0:T(8,128)S(1)} collective-permute-done((f32[12,12,16,128]{3,2,1,0:T(8,128)S(1)}, f32[12,12,16,128]{3,2,1,0:T(8,128)S(1)}, u32[]{:S(2)}, u32[]{:S(2)}) %collective-permute-start.4) | collective-permute-done | bytes 1179680 | tf_op jit(solution)/shard_map/ppermute | solution.py:26
  447.4 26.0 %collective-permute-done.5 = f32[12,12,16,128]{3,2,1,0:T(8,128)S(1)} collective-permute-done((f32[12,12,16,128]{3,2,1,0:T(8,128)S(1)}, f32[12,12,16,128]{3,2,1,0:T(8,128)S(1)}, u32[]{:S(2)}, u32[]{:S(2)}) %collective-permute-start.5) | collective-permute-done | bytes 1179680 | tf_op jit(solution)/shard_map/ppermute | solution.py:26
  473.4 3.0 collective-permute-start.6
  476.4 24.8 %collective-permute-done.6 = f32[12,12,16,128]{3,2,1,0:T(8,128)S(1)} collective-permute-done((f32[12,12,16,128]{3,2,1,0:T(8,128)S(1)}, f32[12,12,16,128]{3,2,1,0:T(8,128)S(1)}, u32[]{:S(2)}, u32[]{:S(2)}) %collective-permute-start.6) | collective-permute-done | bytes 1179680 | tf_op jit(solution)/shard_map/ppermute | solution.py:26
  (36 shorter events, 20.7 us)
Async XLA Ops:
  6.5 10.3 %copy-start = (bf16[12,12,60,128]{3,2,1,0:T(8,128)(2,1)S(1)}, bf16[12,12,60,128]{3,2,1,0:T(8,128)(2,1)}, u32[]{:S(2)}) copy-start(bf16[12,12,60,128]{3,2,1,0:T(8,128)(2,1)} %param.4) | copy-start | bytes 6635524
  6.5 67.9 %copy-start.1 = (s32[4,4]{1,0:T(4,128)S(1)}, s32[4,4]{1,0:T(4,128)}, u32[]{:S(2)}) copy-start(s32[4,4]{1,0:T(4,128)} %param.7) | copy-start | bytes 196
  6.5 144.4 %all-gather.2.cloned.1.call-start = ((), (), s32[]{:S(2)}) async-start(), calls=%async_computation.2 | async-start | bytes 11796480 | tf_op jit(solution)/shard_map/all_gather | solution.py:70
  16.8 320.6 %reduce-scatter.2.cloned.1.call-start = ((), (), s32[]{:S(2)}) async-start(), calls=%async_computation.3 | async-start | bytes 14155776 | tf_op jit(solution)/shard_map/reduce_scatter | solution.py:74
  16.9 54.3 %collective-permute-start = (bf16[12,12,60,128]{3,2,1,0:T(8,128)(2,1)S(1)}, bf16[12,12,60,128]{3,2,1,0:T(8,128)(2,1)}, u32[]{:S(2)}, u32[]{:S(2)}) collective-permute-start(bf16[12,12,60,128]{3,2,1,0:T(8,128)(2,1)S(1)} %copy-done), channel_id=1, source_target_pairs={{0,8},{8,16},{16,24},{24,0},{1,9},{9,17},{17,25},{25,1},{2,10},{10... | collective-permute-start | bytes 6635528 | tf_op jit(solution)/shard_map/ppermute | solution.py:16
  71.2 53.6 %collective-permute-start.1 = (bf16[12,12,60,128]{3,2,1,0:T(8,128)(2,1)}, bf16[12,12,60,128]{3,2,1,0:T(8,128)(2,1)}, u32[]{:S(2)}, u32[]{:S(2)}) collective-permute-start(bf16[12,12,60,128]{3,2,1,0:T(8,128)(2,1)} %collective-permute-done), channel_id=1, source_target_pairs={{0,8},{8,16},{16,24},{24,0},{1,9},{9,17},{17,25},{25,1},{2,10},{10... | collective-permute-start | bytes 6635528 | tf_op jit(solution)/shard_map/ppermute | solution.py:16
  71.6 62.5 %collective-permute-start.2 = (bf16[12,12,60,128]{3,2,1,0:T(8,128)(2,1)S(1)}, bf16[12,12,60,128]{3,2,1,0:T(8,128)(2,1)}, u32[]{:S(2)}, u32[]{:S(2)}) collective-permute-start(bf16[12,12,60,128]{3,2,1,0:T(8,128)(2,1)S(1)} %copy-done), channel_id=1, source_target_pairs={{0,24},{8,0},{16,8},{24,16},{1,25},{9,1},{17,9},{25,17},{2,26},{10... | collective-permute-start | bytes 6635528 | tf_op jit(solution)/shard_map/ppermute | solution.py:18
  415.0 2.9 collective-permute-start.3
  417.9 28.0 %collective-permute-start.4 = (f32[12,12,16,128]{3,2,1,0:T(8,128)S(1)}, f32[12,12,16,128]{3,2,1,0:T(8,128)S(1)}, u32[]{:S(2)}, u32[]{:S(2)}) collective-permute-start(f32[12,12,16,128]{3,2,1,0:T(8,128)S(1)} %collective-permute-done.3), channel_id=1, source_target_pairs={{0,8},{8,0},{16,24},{24,16},{1,9},{9,1},{17,25},{25,17},{2,10},{10... | collective-permute-start | bytes 3538952 | tf_op jit(solution)/shard_map/ppermute | solution.py:26
  446.2 27.2 %collective-permute-start.5 = (f32[12,12,16,128]{3,2,1,0:T(8,128)S(1)}, f32[12,12,16,128]{3,2,1,0:T(8,128)S(1)}, u32[]{:S(2)}, u32[]{:S(2)}) collective-permute-start(f32[12,12,16,128]{3,2,1,0:T(8,128)S(1)} %copy.23), channel_id=1, source_target_pairs={{0,64},{32,96},{64,0},{96,32},{1,65},{33,97},{65,1},{97,33},{2,66}... | collective-permute-start | bytes 3538952 | tf_op jit(solution)/shard_map/ppermute | solution.py:26
  473.4 27.8 %collective-permute-start.6 = (f32[12,12,16,128]{3,2,1,0:T(8,128)S(1)}, f32[12,12,16,128]{3,2,1,0:T(8,128)S(1)}, u32[]{:S(2)}, u32[]{:S(2)}) collective-permute-start(f32[12,12,16,128]{3,2,1,0:T(8,128)S(1)} %collective-permute-done.5), channel_id=1, source_target_pairs={{0,16},{8,24},{16,0},{24,8},{1,17},{9,25},{17,1},{25,9},{2,18},{10... | collective-permute-start | bytes 3538952 | tf_op jit(solution)/shard_map/ppermute | solution.py:26
Sparse Core Ops, SparseCore 0:
  16.9 91.0 all-gather.1
  185.8 151.5 reduce-scatter.1
